TPU v7x, 128 devices: a whole 4x4x4 slice. The times are simulated.
128 devices in a mesh: redist: 32 (over x, y, core), rep: 4 (over z).
Axes of the slice: x: 4, y: 4, z: 4, core: 2. Of those that a mesh axis runs over, the one named last changes fastest.
Arguments:
- amplitudes: bfloat16 [4, 128, 1024, 1024], P(None, ('redist', 'rep')), may hold values from -6 to 6
- integrals: bfloat16 [128, 1024, 2, 1024], P(None, 'redist'), may hold values from -0.046875 to 0.046875
- occ_irrep: int32 [128], replicated, may hold values from 0 to 7, as said below
- virt_irrep: int32 [1024], replicated, may hold values from 0 to 7, as said below
Outputs:
- cycle_term: float32 [4, 1024, 2, 1024], P(None, None, None, 'redist')
Inputs may be any that keep to these rules, and one draw needn't show every extreme that they name: `occ_irrep`: labels never fall along the orbitals; each of the 8 irreps holds one contiguous range of between n // 16 and 3 * n // 16 orbitals, n being 128 or 1024. `virt_irrep`: labels never fall along the orbitals; each of the 8 irreps holds one contiguous range of between n // 16 and 3 * n // 16 orbitals, n being 128 or 1024.
All inputs are finite; a program needn't handle non-finite values.
Results may differ from a plain program's by a relative error of at most 0.0003.
Values may be sent and summed in bfloat16 or wider, within the bound.
No kernel may reach another device: no remote copies, remote signals or barrier semaphores. Data moves between devices by JAX's collectives and lax.ppermute only.
A program may use at most 192 MiB of HBM per device.

v0:
```python
import jax
import jax.numpy as jnp
from jax import lax
from jax.sharding import PartitionSpec as P

N_IRREPS = 8


def irrep_windows(virt_irrep, width):
    count = virt_irrep.shape[0]
    starts = jnp.sum(
        (virt_irrep[None, :] < jnp.arange(N_IRREPS, dtype=virt_irrep.dtype)[:, None]).astype(
            jnp.int32
        ),
        axis=1,
    )
    return jnp.minimum(starts, count - width)


def parts_in(span, count):
    return min(N_IRREPS, -(-span // (count // 16)) + 1)


def body(amplitudes, integrals, occ_irrep, virt_irrep):
    n_redist = lax.axis_size("redist")
    n_rep = lax.axis_size("rep")
    dev_index = lax.axis_index("redist")
    rep_index = lax.axis_index("rep")
    i_slab, k_block, v_width, _ = amplitudes.shape
    c_block = integrals.shape[1]
    j_slab = integrals.shape[2]
    width = 3 * v_width // 16
    wins = irrep_windows(virt_irrep, width)
    occ_rows = occ_irrep[:i_slab]
    occ_js = occ_irrep[:j_slab]
    grouped = integrals.reshape(n_redist, n_rep, k_block, c_block, j_slab, v_width)
    mine = lax.dynamic_index_in_dim(grouped, rep_index, 1, keepdims=False)
    mine = mine.reshape(n_redist * k_block, c_block, j_slab, v_width)
    dest_k = (
        (jnp.arange(n_redist, dtype=jnp.int32)[:, None] * n_rep + rep_index) * k_block
        + jnp.arange(k_block, dtype=jnp.int32)[None, :]
    ).reshape(-1)
    dest_lab = occ_irrep[dest_k]
    c_lab = lax.dynamic_slice_in_dim(virt_irrep, dev_index * c_block, c_block)
    n_cparts = parts_in(c_block, v_width)
    pieces = []
    for d in range(n_redist * k_block):
        row = mine[d]
        piece = jnp.zeros((c_block, j_slab, width), integrals.dtype)
        for p in range(n_cparts):
            lab = jnp.minimum(c_lab[0] + p, N_IRREPS - 1)
            start = wins[jnp.bitwise_xor(lab, dest_lab[d])]
            cut = lax.dynamic_slice_in_dim(row, start, width, axis=2)
            piece = jnp.where((c_lab == c_lab[0] + p)[:, None, None], cut, piece)
        pieces.append(piece)
    packed = jnp.stack(pieces)
    moved = lax.all_to_all(packed, "redist", split_axis=0, concat_axis=1, tiled=True)
    moved = moved.reshape(k_block, n_redist * c_block, j_slab, width)
    my_k0 = (dev_index * n_rep + rep_index) * k_block
    blocks = []
    for kk in range(k_block):
        k_lab = occ_irrep[my_k0 + kk]
        amp = amplitudes[:, kk]
        ints = moved[kk]
        pair_ik = jnp.bitwise_xor(occ_rows, k_lab)
        per_g = []
        for g in range(N_IRREPS):
            c_irrep = jnp.bitwise_xor(g, k_lab)
            wa = wins[g]
            wc = wins[c_irrep]
            a_lab = lax.dynamic_slice_in_dim(virt_irrep, wa, width)
            cw_lab = lax.dynamic_slice_in_dim(virt_irrep, wc, width)
            a_blk = lax.dynamic_slice(amp, (0, wa, wc), (i_slab, width, width))
            allowed = (
                pair_ik[:, None, None] == jnp.bitwise_xor(a_lab[:, None], cw_lab[None, :])[None]
            )
            a_blk = jnp.where(allowed, a_blk, jnp.zeros((), a_blk.dtype))
            i_blk = lax.dynamic_slice_in_dim(ints, wc, width, axis=0)
            sym = (cw_lab == c_irrep)[:, None, None] & (
                jnp.bitwise_xor(cw_lab, k_lab)[:, None, None]
                == jnp.bitwise_xor(occ_js[:, None], a_lab[None, :])[None]
            )
            i_blk = jnp.where(sym, i_blk, jnp.zeros((), i_blk.dtype))
            blk = lax.dot_general(
                i_blk, a_blk, (((0,), (2,)), ((), ())), preferred_element_type=jnp.float32
            )
            per_g.append(jnp.transpose(blk, (1, 0, 2, 3)).reshape(width, -1))
        blocks.append(jnp.concatenate(per_g, axis=0))
    every = blocks[0]
    for more in blocks[1:]:
        every = every + more
    b_pos = jnp.arange(v_width, dtype=jnp.int32)
    pick = virt_irrep * width + (b_pos - wins[virt_irrep])
    compact = jnp.take(every, pick, axis=0)
    shares = lax.psum_scatter(compact, ("redist", "rep"), scatter_dimension=0, tiled=True)
    mine_b = lax.all_gather(shares, "rep", axis=0, tiled=True)
    nb = mine_b.shape[0]
    b_lab = lax.dynamic_slice_in_dim(virt_irrep, dev_index * nb, nb)
    vals = mine_b.reshape(nb, j_slab, i_slab, width).transpose(2, 3, 1, 0)
    out = jnp.zeros((i_slab, v_width, j_slab, nb), jnp.float32)
    for p in range(parts_in(nb, v_width)):
        lab = b_lab[0] + p
        part = jnp.where((b_lab == lab)[None, None, None, :], vals, 0.0)
        start = wins[jnp.minimum(lab, N_IRREPS - 1)]
        placed = lax.dynamic_update_slice(
            jnp.zeros((i_slab, v_width, j_slab, nb), jnp.float32), part, (0, start, 0, 0)
        )
        out = out + placed
    return out


def solution(mesh):
    placed = (P(None, ("redist", "rep"), None, None), P(None, "redist", None, None), P(), P())
    return jax.shard_map(
        body, mesh=mesh, in_specs=placed, out_specs=P(None, None, None, "redist"), check_vma=False
    )
```

profile of v0, /device:TPU:0, one launch (start us, length us, event | category | flops | bytes accessed | tf_op | source)
XLA Modules:
  0.0 598.9 jit_solution(7848239957368478515)
XLA Ops:
  144.4 16.4 %copy.38 = bf16[128,32,2,1024]{3,1,2,0:T(8,128)(2,1)} copy(bf16[128,32,2,1024]{3,2,1,0:T(2,128)(2,1)} %param.5) | data formatting | bytes 33554432 | tf_op args[1]
  200.8 1.6 constant_dynamic-update-slice_fusion.31
  202.4 1.6 constant_dynamic-update-slice_fusion.30
  205.5 1.6 constant_dynamic-update-slice_fusion.28
  207.1 1.6 constant_dynamic-update-slice_fusion.27
  208.7 1.6 constant_dynamic-update-slice_fusion.26
  210.3 1.6 constant_dynamic-update-slice_fusion.25
  211.9 1.6 constant_dynamic-update-slice_fusion.24
  213.5 1.6 constant_dynamic-update-slice_fusion.23
  215.0 1.6 constant_dynamic-update-slice_fusion.22
  240.4 1.6 constant_dynamic-update-slice_fusion.6
  242.0 1.6 constant_dynamic-update-slice_fusion.5
  243.6 1.6 constant_dynamic-update-slice_fusion.4
  251.3 7.1 %all-to-all-start = ((bf16[32,32,2,192]{3,1,2,0:T(8,128)(2,1)}), bf16[32,32,2,192]{3,1,2,0:T(8,128)(2,1)S(1)}, u32[]{:S(2)}, u32[]{:S(2)}) async-start(bf16[32,32,2,192]{3,1,2,0:T(8,128)(2,1)} %constant_dynamic-update-slice_fusion), calls=%async_computation | async-start | bytes 2097152 | tf_op jit(solution)/shard_map/all_to_all | solution.py:57
  278.6 4.9 compare_and_fusion
  300.6 1.7 fusion.4
  303.7 1.6 fusion.1
  306.9 2.4 constant_dynamic-update-slice_fusion.39
  309.3 1.7 fusion.7
  312.4 1.7 fusion.10
  315.6 1.6 fusion.13
  318.7 1.6 fusion.16
  321.9 1.6 fusion.19
  328.0 2.5 constant_dynamic-update-slice_fusion.38
  330.5 2.4 constant_dynamic-update-slice_fusion.37
  332.9 2.4 constant_dynamic-update-slice_fusion.36
  335.3 2.4 constant_dynamic-update-slice_fusion.35
  341.2 11.4 %gather_fusion.1 = f32[1024,1536]{1,0:T(8,128)} fusion(f32[1536,1536]{1,0:T(8,128)} %constant_dynamic-update-slice_fusion.32, s32[1024]{0:T(1024)S(1)} %broadcast_clamp_fusion), kind=kCustom, calls=%fused_computation.1 | custom fusion | bytes 12587008 | tf_op jit(solution)/shard_map/jit(_take)/gather | solution.py:94
  352.6 5.9 broadcast_select_fusion
  362.5 212.3 %reduce-scatter.2.cloned.1.call-done = f32[8,1536]{1,0:T(8,128)} async-done(((f32[1024,1536]{1,0:T(8,128)}), f32[8,1536]{1,0:T(8,128)}) %reduce-scatter.2.cloned.1.call-update) | async-done | bytes 49168 | tf_op jit(solution)/shard_map/reduce_scatter | solution.py:95
  574.7 12.3 %all_gather.3 = f32[32,1536]{1,0:T(8,128)S(1)} all-gather(f32[8,1536]{1,0:T(8,128)} %reduce-scatter.2.cloned.1.call-done), channel_id=1, replica_groups=mesh['redist'=32,'rep'=4] {'rep'}, dimensions={0}, use_global_device_ids=true | all-gather | bytes 245760 | tf_op jit(solution)/shard_map/all_gather | solution.py:96
  589.0 3.0 add.795
  (83 shorter events, 68.1 us)
Async XLA Ops:
  144.4 134.2 %copy-start.6 = (s32[1024]{0:T(1024)S(1)}, s32[1024]{0:T(1024)}, u32[]{:S(2)}) copy-start(s32[1024]{0:T(1024)} %param.7) | copy-start | bytes 12292
  144.4 153.6 %copy-start = (s32[128]{0:T(128)S(1)}, s32[128]{0:T(128)}, u32[]{:S(2)}) copy-start(s32[128]{0:T(128)} %param.6) | copy-start | bytes 1540
  251.3 49.2 %all-to-all-start = ((bf16[32,32,2,192]{3,1,2,0:T(8,128)(2,1)}), bf16[32,32,2,192]{3,1,2,0:T(8,128)(2,1)S(1)}, u32[]{:S(2)}, u32[]{:S(2)}) async-start(bf16[32,32,2,192]{3,1,2,0:T(8,128)(2,1)} %constant_dynamic-update-slice_fusion), calls=%async_computation | async-start | bytes 2097152 | tf_op jit(solution)/shard_map/all_to_all | solution.py:57
  258.4 316.3 %reduce-scatter.2.cloned.1.call-start = ((), (), s32[]{:S(2)}) async-start(), calls=%async_computation.2 | async-start | bytes 6340608 | tf_op jit(solution)/shard_map/reduce_scatter | solution.py:95
  305.4 10.2 %copy-start.5 = (s32[192,192]{1,0:T(8,128)S(1)}, s32[192,192]{1,0:T(8,128)}, u32[]{:S(2)}) copy-start(s32[192,192]{1,0:T(8,128)} %get-tuple-element.180) | copy-start | bytes 442372
  328.0 9.7 %copy-start.1 = (f32[192,1536]{1,0:T(8,128)S(1)}, f32[192,1536]{1,0:T(8,128)}, u32[]{:S(2)}) copy-start(f32[192,1536]{1,0:T(8,128)} %copy.45) | copy-start | bytes 3538948
  328.0 10.8 %copy-start.2 = (f32[192,1536]{1,0:T(8,128)S(1)}, f32[192,1536]{1,0:T(8,128)}, u32[]{:S(2)}) copy-start(f32[192,1536]{1,0:T(8,128)} %copy.46) | copy-start | bytes 3538948
  328.0 11.9 %copy-start.3 = (f32[192,1536]{1,0:T(8,128)S(1)}, f32[192,1536]{1,0:T(8,128)}, u32[]{:S(2)}) copy-start(f32[192,1536]{1,0:T(8,128)} %copy.47) | copy-start | bytes 3538948
  588.1 1.0 copy-start.4
Sparse Core Ops, SparseCore 0:
  358.7 216.0 reduce-scatter.1
where the time goes:
time: 605 us; the launch traced here: 599 us
  between operations  215 us (36%)
  waiting for transfers between devices  212 us (35%)
  other arithmetic  70.2 us (12%)
  local copies, waits for them, and re-layouts  69 us (11%)
  matrix products  13 us (2%)
  blocking collectives  12.3 us (2%)
  starting transfers between devices  7.32 us (1%)
    reduce_scatter x1, waiting for transfers between devices, body(): lax.psum_scatter(compact, ('redist', 'rep'), scatter_dimension=0, tiled=T...  212 us
    unnamed x31, other arithmetic  49 us
    unnamed x22, local copies, waits for them, and re-layouts  31.6 us
    dot_general x8, matrix products, body(): lax.dot_general(i_blk, a_blk, (((0,), (2,)), ((), ())), preferred_element...  13 us
    all_gather x1, blocking collectives, body(): mine_b = lax.all_gather(shares, 'rep', axis=0, tiled=True)  12.3 us
  transfers between devices with their start and end apart: 2, of which 1 were waited for; matrix products, arithmetic and copies ran while one was open for 2% of the time, Pallas kernels for 0%

commit v1 on v0

--- a/solution.py
+++ b/solution.py
@@ -93,7 +93,9 @@
     pick = virt_irrep * width + (b_pos - wins[virt_irrep])
     compact = jnp.take(every, pick, axis=0)
     shares = lax.psum_scatter(compact, ("redist", "rep"), scatter_dimension=0, tiled=True)
-    mine_b = lax.all_gather(shares, "rep", axis=0, tiled=True)
+    mine_b = jnp.concatenate(
+        lax.all_to_all(jnp.stack([shares] * lax.axis_size("rep")), "rep", 0, 0), axis=0
+    )
     nb = mine_b.shape[0]
     b_lab = lax.dynamic_slice_in_dim(virt_irrep, dev_index * nb, nb)
     vals = mine_b.reshape(nb, j_slab, i_slab, width).transpose(2, 3, 1, 0)

time: 605 us -> 622 us (1.028)
  the two profiles are of different devices: /device:TPU:0 before, /device:TPU:2 now
where the time goes in v1:
time: 622 us; the launch traced here: 616 us
  waiting for transfers between devices  217 us (35%)
  between operations  215 us (35%)
  local copies, waits for them, and re-layouts  90 us (14%)
  other arithmetic  70.2 us (11%)
  matrix products  13 us (2%)
  starting transfers between devices  11.4 us (2%)
    reduce_scatter x1, waiting for transfers between devices, body(): lax.psum_scatter(compact, ('redist', 'rep'), scatter_dimension=0, tiled=T...  215 us
    unnamed x31, other arithmetic  48.6 us
    unnamed x20, local copies, waits for them, and re-layouts  30.8 us
    dot_general x8, matrix products, body(): lax.dot_general(i_blk, a_blk, (((0,), (2,)), ((), ())), preferred_element...  13 us
    add x2, local copies, waits for them, and re-layouts, body(): out = out + placed  12.7 us
  transfers between devices with their start and end apart: 3, of which 2 were waited for; matrix products, arithmetic and copies ran while one was open for 2% of the time, Pallas kernels for 0%

profile of v1, /device:TPU:2, one launch (start us, length us, event | category | flops | bytes accessed | tf_op | source)
XLA Modules:
  0.0 616.1 jit_solution(8289112720962594651)
XLA Ops:
  144.0 16.5 %copy.34 = bf16[128,32,2,1024]{3,1,2,0:T(8,128)(2,1)} copy(bf16[128,32,2,1024]{3,2,1,0:T(2,128)(2,1)} %param.5) | data formatting | bytes 33554432 | tf_op args[1]
  200.2 1.6 constant_dynamic-update-slice_fusion.31
  201.8 1.6 constant_dynamic-update-slice_fusion.30
  203.4 1.6 constant_dynamic-update-slice_fusion.29
  205.0 1.6 constant_dynamic-update-slice_fusion.28
  206.5 1.6 constant_dynamic-update-slice_fusion.27
  208.1 1.6 constant_dynamic-update-slice_fusion.26
  209.7 1.6 constant_dynamic-update-slice_fusion.25
  211.3 1.6 constant_dynamic-update-slice_fusion.24
  212.9 1.6 constant_dynamic-update-slice_fusion.23
  224.0 1.6 constant_dynamic-update-slice_fusion.16
  250.4 7.6 %all-to-all-start = ((bf16[32,32,2,192]{3,1,2,0:T(8,128)(2,1)}), bf16[32,32,2,192]{3,1,2,0:T(8,128)(2,1)S(1)}, u32[]{:S(2)}, u32[]{:S(2)}) async-start(bf16[32,32,2,192]{3,1,2,0:T(8,128)(2,1)} %constant_dynamic-update-slice_fusion), calls=%async_computation | async-start | bytes 2097152 | tf_op jit(solution)/shard_map/all_to_all | solution.py:57
  278.5 5.2 compare_and_fusion
  300.9 1.7 fusion.4
  304.1 1.6 fusion.1
  307.2 2.4 constant_dynamic-update-slice_fusion.39
  309.6 1.7 fusion.7
  312.7 1.6 fusion.10
  315.9 1.6 fusion.13
  319.0 1.6 fusion.16
  325.2 1.6 fusion.22
  328.3 2.5 constant_dynamic-update-slice_fusion.38
  330.8 2.4 constant_dynamic-update-slice_fusion.37
  333.2 2.4 constant_dynamic-update-slice_fusion.36
  335.6 2.4 constant_dynamic-update-slice_fusion.35
  341.5 11.4 %gather_fusion.1 = f32[1024,1536]{1,0:T(8,128)} fusion(f32[1536,1536]{1,0:T(8,128)} %constant_dynamic-update-slice_fusion.32, s32[1024]{0:T(1024)S(1)} %broadcast_clamp_fusion), kind=kCustom, calls=%fused_computation.1 | custom fusion | bytes 12587008 | tf_op jit(solution)/shard_map/jit(_take)/gather | solution.py:94
  352.9 5.9 broadcast_select_fusion
  358.8 214.6 %reduce-scatter.2.cloned.1.call-done = f32[8,1536]{1,0:T(8,128)} async-done(((f32[1024,1536]{1,0:T(8,128)}), f32[8,1536]{1,0:T(8,128)}) %reduce-scatter.2.cloned.1.call-update) | async-done | bytes 49168 | tf_op jit(solution)/shard_map/reduce_scatter | solution.py:95
  574.9 3.6 all-to-all-start.1
  582.3 2.3 all-to-all-done.1
  585.2 11.1 %dynamic_update_slice.8 = f32[4,1024,2,32]{1,0,2,3:T(4,128)S(1)} dynamic-update-slice(f32[4,1024,2,32]{1,0,2,3:T(4,128)S(1)} %broadcast.1051, f32[4,192,2,32]{1,0,2,3:T(4,128)S(1)} %select_bitcast_fusion, s32[]{:T(128)} %constant.121.clone.1, s32[]{:T(128)S(6)} %select_n.1471, s32[]{:T(128)} %constant.121.clone.1, s32[]{:T(128)} %constant.121.clone.1) | dynamic-update-slice | bytes 393220 | tf_op jit(solution)/shard_map/dynamic_update_slice | solution.py:107
  596.6 11.1 %add.795 = f32[4,1024,2,32]{1,0,2,3:T(4,128)S(1)} dynamic-update-slice(f32[4,1024,2,32]{1,0,2,3:T(4,128)S(1)} %dynamic_update_slice.8, f32[4,192,2,32]{1,0,2,3:T(4,128)S(1)} %bitcast_add_fusion, s32[]{:T(128)} %constant.121.clone.1, s32[]{:T(128)S(6)} %select_n.1473, s32[]{:T(128)} %constant.121.clone.1, s32[]{:T(128)} %constant.121.clone.1) | dynamic-update-slice | bytes 393220 | tf_op jit(solution)/shard_map/add | solution.py:110
  (84 shorter events, 72.8 us)
Async XLA Ops:
  143.9 134.5 %copy-start.5 = (s32[1024]{0:T(1024)S(1)}, s32[1024]{0:T(1024)}, u32[]{:S(2)}) copy-start(s32[1024]{0:T(1024)} %param.7) | copy-start | bytes 12292
  144.0 154.3 %copy-start = (s32[128]{0:T(128)S(1)}, s32[128]{0:T(128)}, u32[]{:S(2)}) copy-start(s32[128]{0:T(128)} %param.6) | copy-start | bytes 1540
  250.4 50.4 %all-to-all-start = ((bf16[32,32,2,192]{3,1,2,0:T(8,128)(2,1)}), bf16[32,32,2,192]{3,1,2,0:T(8,128)(2,1)S(1)}, u32[]{:S(2)}, u32[]{:S(2)}) async-start(bf16[32,32,2,192]{3,1,2,0:T(8,128)(2,1)} %constant_dynamic-update-slice_fusion), calls=%async_computation | async-start | bytes 2097152 | tf_op jit(solution)/shard_map/all_to_all | solution.py:57
  258.1 315.4 %reduce-scatter.2.cloned.1.call-start = ((), (), s32[]{:S(2)}) async-start(), calls=%async_computation.3 | async-start | bytes 6340608 | tf_op jit(solution)/shard_map/reduce_scatter | solution.py:95
  305.7 10.2 %copy-start.4 = (s32[192,192]{1,0:T(8,128)S(1)}, s32[192,192]{1,0:T(8,128)}, u32[]{:S(2)}) copy-start(s32[192,192]{1,0:T(8,128)} %get-tuple-element.180) | copy-start | bytes 442372
  328.3 9.6 %copy-start.1 = (f32[192,1536]{1,0:T(8,128)S(1)}, f32[192,1536]{1,0:T(8,128)}, u32[]{:S(2)}) copy-start(f32[192,1536]{1,0:T(8,128)} %copy.41) | copy-start | bytes 3538948
  328.3 10.8 %copy-start.2 = (f32[192,1536]{1,0:T(8,128)S(1)}, f32[192,1536]{1,0:T(8,128)}, u32[]{:S(2)}) copy-start(f32[192,1536]{1,0:T(8,128)} %copy.42) | copy-start | bytes 3538948
  328.3 11.9 %copy-start.3 = (f32[192,1536]{1,0:T(8,128)S(1)}, f32[192,1536]{1,0:T(8,128)}, u32[]{:S(2)}) copy-start(f32[192,1536]{1,0:T(8,128)} %copy.43) | copy-start | bytes 3538948
  574.9 9.7 %all-to-all-start.1 = ((f32[4,8,1536]{2,1,0:T(8,128)}), f32[4,8,1536]{2,1,0:T(8,128)S(1)}, u32[]{:S(2)}, u32[]{:S(2)}) async-start(f32[4,8,1536]{2,1,0:T(8,128)} %stack.5), calls=%async_computation.2 | async-start | bytes 393216 | tf_op jit(solution)/shard_map/all_to_all | solution.py:97
Sparse Core Ops, SparseCore 0:
  359.0 214.4 reduce-scatter.1
